TPU v7x, 32 devices: a whole 2x2x4 slice. The times are simulated.
32 devices in a mesh: req: 4 (over y, x), exp: 4 (over z), ffn: 2 (over core).
Axes of the slice: x: 2, y: 2, z: 4, core: 2. Of those that a mesh axis runs over, the one named last changes fastest.
Arguments:
- residual: bfloat16 [2048, 2048], P(('req', 'exp')), may hold values from -5 to 5
- queries: bfloat16 [2048, 4608], P(('req', 'exp'), 'ffn'), may hold values from -30 to 30
- new_latent: bfloat16 [2048, 576], P(('req', 'exp')), may hold values from -6 to 6
- cache_pool: bfloat16 [512, 9216], P(('req', 'exp')), may hold values from -5 to 5
- page_table: int32 [8, 64], replicated, may hold values from 0 to 511, as said below
- cached_len: int32 [8], replicated, may hold values from 0 to 1024
- tenant_start: int32 [8], replicated, may hold values from 0 to 512, as said below
- routes: int32 [2048, 6], P(('req', 'exp')), may hold values from 0 to 31, all different within a row; in each aligned block of 64 rows (0 to 63, 64 to 127, ...) at most 16 rows name the same one
- value_up: bfloat16 [512, 1024], P(None, 'ffn'), may hold values from -0.25 to 0.25
- out_proj: bfloat16 [1024, 2048], P('ffn'), may hold values from -0.1875 to 0.1875
- norm_gain: bfloat16 [2048], replicated, may hold values from 0.099609375 to 1.8984375
- router: bfloat16 [2048, 32], replicated, may hold values from -0.125 to 0.125
- gate_weight: bfloat16 [32, 2048, 1408], P('exp', None, 'ffn'), may hold values from -0.125 to 0.125
- up_weight: bfloat16 [32, 2048, 1408], P('exp', None, 'ffn'), may hold values from -0.125 to 0.125
- down_weight: bfloat16 [32, 1408, 2048], P('exp', 'ffn'), may hold values from -0.15625 to 0.15625
Outputs:
- hidden_out: bfloat16 [2048, 2048], P(('req', 'exp'), 'ffn')
- moe_out: bfloat16 [2048, 2048], P(('req', 'exp'), 'ffn')
Inputs may be any that keep to these rules, and one draw needn't show every extreme that they name: `page_table`: row i lists, in order, the pool pages of request i's cache; the 2 requests of group g = i // 2 use pool pages g * 2 * 64 to (g + 1) * 2 * 64 - 1, each exactly once. tenant_start[i] is at most half of cached_len[i]. `routes`: A row names 6 different experts; in each aligned block of 64 rows at most 16 rows name the same expert.
All inputs are finite; a program needn't handle non-finite values.
Results may differ from a plain program's by a relative error of at most 0.025.
Values may be sent and summed in bfloat16 or wider, within the bound.
No kernel may reach another device: no remote copies, remote signals or barrier semaphores. Data moves between devices by JAX's collectives and lax.ppermute only.
A program may use at most 128 MiB of HBM per device.

v0:
```python
import jax
import jax.numpy as jnp
from jax import lax
from jax.sharding import PartitionSpec as P

LATENT = 512
ROPE_DIM = 64
HEAD_DIM = 128
QKD = 576
EXPERTS = 32
TOP = 6
CAPACITY = 16
REQ_GRP = 2
CMAX = 1024
BLOCK_ROWS = 64
EPSILON = 1e-06
NEG_FILL = -1e30


def slot_numbers(route_block):
    expert_ids = lax.broadcasted_iota(jnp.int32, (1, EXPERTS), 1)
    onehot = (route_block[:, None] == expert_ids).astype(jnp.int32)
    before = jnp.cumsum(onehot, axis=0) - onehot
    return jnp.sum(before * onehot, axis=1)


def local(
    residual,
    queries,
    new_latent,
    cache_pool,
    page_table,
    cached_len,
    tenant_start,
    routes,
    value_up,
    out_proj,
    norm_gain,
    router,
    gate_weight,
    up_weight,
    down_weight,
):
    exp_size = lax.axis_size("exp")
    ffn_size = lax.axis_size("ffn")
    req_index = lax.axis_index("req")
    exp_index = lax.axis_index("exp")
    ffn_index = lax.axis_index("ffn")
    token_rows = residual.shape[0]
    feature_count = residual.shape[1]
    fresh_len = token_rows * exp_size // REQ_GRP
    first_token = (req_index * exp_size + exp_index) * token_rows
    request = first_token // fresh_len
    offset = first_token - request * fresh_len
    pool_all, latent_all = (
        lax.all_gather(cache_pool, "exp", axis=0, tiled=True),
        lax.all_gather(new_latent, "exp", axis=0, tiled=True),
    )
    pool_base = req_index * pool_all.shape[0]
    page_rows = page_table[request] - pool_base
    cached_keys = jnp.take(pool_all, page_rows, axis=0).reshape(CMAX, QKD)
    local_request = request - req_index * REQ_GRP
    fresh_keys = lax.dynamic_slice_in_dim(latent_all, local_request * fresh_len, fresh_len, 0)
    all_keys = jnp.concatenate([cached_keys, fresh_keys], axis=0)
    heads_here = queries.shape[1] // QKD
    query_heads = queries.reshape(token_rows, heads_here, QKD)
    scale_factor = (HEAD_DIM + ROPE_DIM) ** (-0.5)
    scores = (
        jnp.einsum("thd,kd->thk", query_heads, all_keys, preferred_element_type=jnp.float32)
        * scale_factor
    )
    key_pos = lax.broadcasted_iota(jnp.int32, (1, CMAX + fresh_len), 1)
    tok_pos = offset + lax.broadcasted_iota(jnp.int32, (token_rows, 1), 0)
    cached_ok = (key_pos >= tenant_start[request]) & (key_pos < cached_len[request])
    fresh_ok = (key_pos >= CMAX) & (key_pos - CMAX <= tok_pos)
    visible = cached_ok | fresh_ok
    scores = jnp.where(visible[:, None, :], scores, NEG_FILL)
    top_score = jnp.max(scores, axis=2, keepdims=True)
    weights = jnp.exp(scores - top_score)
    attn_probs = (weights / jnp.sum(weights, axis=2, keepdims=True)).astype(jnp.bfloat16)
    latent_out = jnp.einsum(
        "thk,kl->thl", attn_probs, all_keys[:, :LATENT], preferred_element_type=jnp.float32
    ).astype(jnp.bfloat16)
    value_heads = value_up.reshape(LATENT, heads_here, HEAD_DIM)
    head_out = jnp.einsum(
        "thl,lhd->thd", latent_out, value_heads, preferred_element_type=jnp.float32
    )
    head_out = head_out.astype(jnp.bfloat16).reshape(token_rows, heads_here * HEAD_DIM)
    partial_value = jnp.dot(head_out, out_proj, preferred_element_type=jnp.float32)
    column_count = feature_count // ffn_size
    attn_cols = lax.psum_scatter(
        partial_value.astype(jnp.bfloat16), "ffn", scatter_dimension=1, tiled=True
    ).astype(jnp.float32)
    residual_cols = lax.dynamic_slice_in_dim(residual, ffn_index * column_count, column_count, 1)
    hidden_out = (residual_cols.astype(jnp.float32) + attn_cols).astype(jnp.bfloat16)
    hidden_wide = hidden_out.astype(jnp.float32)
    square_sum = lax.psum(jnp.sum(hidden_wide * hidden_wide, axis=1, keepdims=True), "ffn")
    mean_square = square_sum / feature_count
    gain_cols = lax.dynamic_slice_in_dim(norm_gain, ffn_index * column_count, column_count, 0)
    normed_cols = (
        hidden_wide * lax.rsqrt(mean_square + EPSILON) * gain_cols.astype(jnp.float32)
    ).astype(jnp.bfloat16)
    normed_grid = lax.all_gather(normed_cols, ("exp", "ffn"), axis=0, tiled=False)
    normed_grid = normed_grid.reshape(exp_size, ffn_size, token_rows, column_count)
    group_rows = exp_size * token_rows
    routes_all = lax.all_gather(routes, "exp", axis=0, tiled=True)
    logits = jnp.einsum(
        "efrc,fck->erk",
        normed_grid,
        router.reshape(ffn_size, column_count, EXPERTS),
        preferred_element_type=jnp.float32,
    ).reshape(group_rows, EXPERTS)
    chosen = jnp.take_along_axis(logits, routes_all, axis=1)
    raised = jnp.exp(chosen)
    gate_weights = raised / jnp.sum(raised, axis=1, keepdims=True)
    blocks = group_rows // BLOCK_ROWS
    slot_within = jax.vmap(slot_numbers)(routes_all.reshape(blocks, BLOCK_ROWS * TOP))
    block_base = lax.broadcasted_iota(jnp.int32, (blocks, 1), 0) * CAPACITY
    slot_index = (slot_within + block_base).reshape(group_rows * TOP)
    slot_count = blocks * CAPACITY
    local_count = gate_weight.shape[0]
    total_slots = local_count * slot_count
    local_expert = routes_all.reshape(group_rows * TOP) - exp_index * local_count
    is_local = (local_expert >= 0) & (local_expert < local_count)
    local_target = jnp.where(is_local, local_expert * slot_count + slot_index, total_slots)
    token_ids = lax.broadcasted_iota(jnp.int32, (group_rows, TOP), 0).reshape(group_rows * TOP)
    slot_token = jnp.zeros((total_slots,), jnp.int32).at[local_target].set(token_ids, mode="drop")
    slot_weight = (
        jnp.zeros((total_slots,), jnp.float32)
        .at[local_target]
        .set(gate_weights.reshape(group_rows * TOP), mode="drop")
    )
    grouped = normed_grid[slot_token // token_rows, :, slot_token % token_rows, :]
    grouped = grouped.reshape(local_count, slot_count, feature_count)
    gate_part = jnp.einsum("jmd,jdf->jmf", grouped, gate_weight, preferred_element_type=jnp.float32)
    up_part = jnp.einsum("jmd,jdf->jmf", grouped, up_weight, preferred_element_type=jnp.float32)
    active = (jax.nn.silu(gate_part) * up_part).astype(jnp.bfloat16)
    outputs = jnp.einsum("jmf,jfd->jmd", active, down_weight, preferred_element_type=jnp.float32)
    weighted = (outputs.reshape(total_slots, feature_count) * slot_weight[:, None]).astype(
        jnp.bfloat16
    )
    row_ids = lax.broadcasted_iota(jnp.int32, (group_rows, 1), 0)
    onehot = (slot_token[None, :] == row_ids).astype(jnp.bfloat16)
    mixture = jnp.einsum(
        "ers,sfc->efrc",
        onehot.reshape(exp_size, token_rows, total_slots),
        weighted.reshape(total_slots, ffn_size, column_count),
        preferred_element_type=jnp.float32,
    ).astype(jnp.bfloat16)
    mixture = mixture.reshape(exp_size * ffn_size * token_rows, column_count)
    moe_out = lax.psum_scatter(mixture, ("exp", "ffn"), scatter_dimension=0, tiled=True)
    return (hidden_out, moe_out)


def solution(mesh):
    in_specs = (
        P(("req", "exp"), None),
        P(("req", "exp"), "ffn"),
        P(("req", "exp"), None),
        P(("req", "exp"), None),
        P(),
        P(),
        P(),
        P(("req", "exp"), None),
        P(None, "ffn"),
        P("ffn", None),
        P(),
        P(),
        P("exp", None, "ffn"),
        P("exp", None, "ffn"),
        P("exp", "ffn", None),
    )
    out_specs = (P(("req", "exp"), "ffn"), P(("req", "exp"), "ffn"))
    return jax.shard_map(local, mesh=mesh, in_specs=in_specs, out_specs=out_specs, check_vma=False)
```

profile of v0, /device:TPU:0, one launch (start us, length us, event | category | flops | bytes accessed | tf_op | source)
XLA Modules:
  0.0 305.1 jit_solution(3223588927788097875)
XLA Ops:
  8.0 2.0 copy.36
  10.9 2.1 copy.24
  16.3 31.2 %all_gather.16 = bf16[512,576]{0,1:T(8,128)(2,1)S(1)} all-gather(bf16[128,576]{0,1:T(8,128)(2,1)S(1)} %copy-done.4), channel_id=1, replica_groups=mesh['req'=4,'exp'=4,'ffn'=2] {'exp'}, dimensions={0}, use_global_device_ids=true | all-gather | bytes 737280 | tf_op jit(solution)/shard_map/all_gather | solution.py:57
  49.9 21.1 %all-gather.4.cloned.1.call-done = bf16[128,9216]{1,0:T(8,128)(2,1)} async-done(((bf16[32,9216]{1,0:T(8,128)(2,1)}), bf16[128,9216]{1,0:T(8,128)(2,1)}) %all-gather.4.cloned.1.call-update) | async-done | bytes 2359312 | tf_op jit(solution)/shard_map/all_gather | solution.py:56
  70.9 5.3 %gather_fusion = bf16[64,9216]{1,0:T(8,128)(2,1)} fusion(bf16[128,9216]{1,0:T(8,128)(2,1)} %all-gather.4.cloned.1.call-done, s32[1024]{0:T(1024)S(1)} %pad_clamp_fusion), kind=kCustom, calls=%fused_computation | custom fusion | bytes 2359552 | tf_op jit(solution)/shard_map/jit(_take)/gather | solution.py:61
  76.3 2.2 gather.14
  81.4 3.0 fusion.72
  84.4 3.9 %fusion.5 = f32[128,4,1280]{0,2,1:T(8,128)} fusion(bf16[128,4,576]{0,2,1:T(8,128)(2,1)} %bitcast.110, bf16[256,576]{0,1:T(8,128)(2,1)} %constant_dynamic-slice_fusion, bf16[1024,576]{0,1:T(8,128)(2,1)S(1)} %broadcast_select_fusion, pred[128,1280]{0,1:T(8,128)(4,1)S(1)} %copy-done.3), kind=kOutput, calls=%fused_computation.12 | convolution fusion | flops 759234560 | bytes 4849664 | tf_op jit(solution)/shard_map/thd,kd->thk/dot_general | solution.py:69
  88.3 3.9 %fusion.27 = bf16[4,128,128]{1,2,0:T(8,128)(2,1)S(1)} fusion(bf16[512,4,128]{0,2,1:T(8,128)(2,1)} %bitcast.111, bf16[1024,576]{0,1:T(8,128)(2,1)S(1)} %broadcast_select_fusion, bf16[256,576]{0,1:T(8,128)(2,1)} %constant_dynamic-slice_fusion, f32[128,4]{0,1:T(4,128)S(1)} %fusion.72, f32[128,4,1280]{0,2,1:T(8,128)} %fusion.5), kind=kOutput, calls=%fused_computation.32 | convolution fusion | flops 743114496 | bytes 7374848 | tf_op jit(solution)/shard_map/thl,lhd->thd/dot_general | solution.py:85
  93.6 7.0 %reduce-scatter.3.cloned.1.call-done = bf16[128,1024]{1,0:T(8,128)(2,1)} async-done(((bf16[128,2048]{1,0:T(8,128)(2,1)}), bf16[128,1024]{1,0:T(8,128)(2,1)}) %reduce-scatter.3.cloned.1.call-update) | async-done | bytes 262160 | tf_op jit(solution)/shard_map/reduce_scatter | solution.py:91
  101.8 2.5 psum.7
  105.3 15.2 %all_gather.19 = s32[512,6]{1,0:T(8,128)S(1)} all-gather(s32[128,6]{1,0:T(8,128)S(1)} %copy.26), channel_id=1, replica_groups=mesh['req'=4,'exp'=4,'ffn'=2] {'exp'}, dimensions={0}, use_global_device_ids=true | all-gather | bytes 15360 | tf_op jit(solution)/shard_map/all_gather | solution.py:106
  121.4 6.9 %reduce-window.6 = s32[8,32,3,128]{3,1,2,0:T(8,128)S(1)} reduce-window(s32[8,32,3,128]{3,1,2,0:T(8,128)S(1)} %fusion.38, s32[]{:T(128)} %constant.65.clone.1), window={size=1x1x1x128 pad=0_0x0_0x0_0x127_0}, to_apply=%region_5.6 | reduce-window | flops 12484608 | bytes 786436 | tf_op jit(solution)/shard_map/reduce-window
  129.7 11.8 %scatter_custom_fusion = s32[1024]{0:T(1024)S(1)} fusion(s32[3072]{0:T(1024)S(1)} %bitcast.115, s32[3072]{0:T(1024)S(1)} %reshape.307, s32[]{:T(128)} %constant.65.clone.1), kind=kCustom, calls=%fused_computation.89 | custom fusion | bytes 4100 | tf_op jit(solution)/shard_map/scatter | solution.py:127
  144.0 24.9 %gather_fusion.2 = f32[3072]{0:T(1024)S(1)} fusion(f32[512,32]{0,1:T(8,128)S(1)} %convolution_bitcast_fusion, s32[3072]{0:T(1024)S(1)} %reshape.297), kind=kCustom, calls=%fused_computation.2 | custom fusion | bytes 49152 | tf_op jit(solution)/shard_map/jit(take_along_axis)/gather | solution.py:113
  169.6 5.1 %copy.30 = bf16[4,2,128,1024]{3,1,2,0:T(2,128)(2,1)} copy(bf16[4,2,128,1024]{3,2,1,0:T(8,128)(2,1)} %bitcast.105) | data formatting | bytes 4194304 | tf_op jit(solution)/shard_map/reshape | solution.py:104
  174.7 18.4 %gather_fusion.1 = bf16[1024,2,1024]{2,1,0:T(2,128)(2,1)} fusion(bf16[4,2,128,1024]{3,1,2,0:T(2,128)(2,1)} %copy.30, s32[1024]{0:T(1024)S(1)} %fusion.49), kind=kCustom, calls=%fused_computation.1 | custom fusion | bytes 8396800 | tf_op jit(solution)/shard_map/gather | solution.py:133
  193.2 7.8 %reshape.279 = bf16[8,128,2048]{2,1,0:T(8,128)(2,1)} reshape(bf16[1024,2,1024]{2,1,0:T(2,128)(2,1)} %gather_fusion.1) | data formatting | bytes 8388608 | tf_op jit(solution)/shard_map/reshape | solution.py:134
  201.0 12.0 %scatter_custom_fusion.1 = f32[1024]{0:T(1024)S(1)} fusion(s32[3072]{0:T(1024)S(1)} %bitcast.116, f32[3072]{0:T(1024)S(1)} %reshape.315, f32[]{:T(128)} %constant.118.clone.1), kind=kCustom, calls=%fused_computation.92 | custom fusion | bytes 4100 | tf_op jit(solution)/shard_map/scatter | solution.py:131
  213.0 13.1 %fusion.75 = f32[8,128,704]{1,2,0:T(8,128)} fusion(bf16[8,128,2048]{2,1,0:T(8,128)(2,1)} %reshape.279, bf16[8,2048,704]{1,2,0:T(8,128)(2,1)} %param.27), kind=kOutput, calls=%fused_computation.111 | convolution fusion | flops 2952790016 | bytes 30146560 | tf_op jit(solution)/shard_map/jmd,jdf->jmf/dot_general | solution.py:135
  226.1 20.7 %multiply_convert_fusion = bf16[8,128,2048]{2,1,0:T(8,128)(2,1)} fusion(f32[8,128]{1,0:T(8,128)S(1)} %bitcast.117, bf16[8,704,2048]{2,1,0:T(8,128)(2,1)} %param.29, f32[8,128,704]{1,2,0:T(8,128)} %fusion.75, bf16[8,128,2048]{2,1,0:T(8,128)(2,1)} %reshape.279, bf16[8,2048,704]{1,2,0:T(8,128)(2,1)} %param.28), kind=kOutput, calls=%fused_computation.6 | convolution fusion | flops 5914099712 | bytes 57413632 | tf_op jit(solution)/shard_map/jmf,jfd->jmd/dot_general | solution.py:138
  246.8 7.8 %convert_element_type.72 = bf16[1024,2,1024]{2,1,0:T(2,128)(2,1)} reshape(bf16[8,128,2048]{2,1,0:T(8,128)(2,1)} %multiply_convert_fusion) | data formatting | bytes 8388608 | tf_op jit(solution)/shard_map/convert_element_type | solution.py:139
  254.6 4.8 %convert_bitcast_fusion = bf16[4,2,128,1024]{3,2,0,1:T(8,128)(2,1)S(1)} fusion(bf16[1024,2,1024,1]{2,1,0,3:T(2,128)(2,1)} %bitcast.108, s32[4,128]{1,0:T(4,128)S(1)} %multiply_add_fusion, s32[1024]{0:T(1024)S(1)} %scatter_custom_fusion), kind=kOutput, calls=%fused_computation.17 | convolution fusion | flops 2149056512 | bytes 6297600 | tf_op jit(solution)/shard_map/ers,sfc->efrc/dot_general | solution.py:144
  261.0 37.6 %reduce-scatter.5.cloned.1.call-done = bf16[128,1024]{1,0:T(8,128)(2,1)} async-done(((bf16[1024,1024]{1,0:T(8,128)(2,1)}), bf16[128,1024]{1,0:T(8,128)(2,1)}) %reduce-scatter.5.cloned.1.call-update) | async-done | bytes 262160 | tf_op jit(solution)/shard_map/reduce_scatter | solution.py:151
  (81 shorter events, 20.5 us)
Async XLA Ops:
  7.2 85.1 %copy-start = (bf16[512,2048]{1,0:T(8,128)(2,1)S(1)}, bf16[512,2048]{1,0:T(8,128)(2,1)}, u32[]{:S(2)}) copy-start(bf16[512,2048]{1,0:T(8,128)(2,1)} %param.24) | copy-start | bytes 6291460
  7.2 5.9 %copy-start.9 = (s32[8]{0:T(128)S(1)}, s32[8]{0:T(128)}, u32[]{:S(2)}) copy-start(s32[8]{0:T(128)} %param.20) | copy-start | bytes 100
  7.2 6.5 %copy-start.10 = (s32[8]{0:T(128)S(1)}, s32[8]{0:T(128)}, u32[]{:S(2)}) copy-start(s32[8]{0:T(128)} %param.21) | copy-start | bytes 100
  7.2 9.1 %copy-start.4 = (bf16[128,576]{0,1:T(8,128)(2,1)S(1)}, bf16[128,576]{0,1:T(8,128)(2,1)}, u32[]{:S(2)}) copy-start(bf16[128,576]{0,1:T(8,128)(2,1)} %param.17) | copy-start | bytes 442372
  7.2 63.7 %all-gather.4.cloned.1.call-start = ((), (), s32[]{:S(2)}) async-start(), calls=%async_computation.2 | async-start | bytes 2949120 | tf_op jit(solution)/shard_map/all_gather | solution.py:56
  7.9 92.7 %reduce-scatter.3.cloned.1.call-start = ((), (), s32[]{:S(2)}) async-start(), calls=%async_computation.3 | async-start | bytes 786432 | tf_op jit(solution)/shard_map/reduce_scatter | solution.py:91
  81.4 3.0 copy-start.3
  92.2 1.4 copy-start.8
  92.2 8.4 %copy-start.6 = (bf16[128,2048]{1,0:T(8,128)(2,1)S(1)}, bf16[128,2048]{1,0:T(8,128)(2,1)}, u32[]{:S(2)}) copy-start(bf16[128,2048]{1,0:T(8,128)(2,1)} %param.15) | copy-start | bytes 1572868
  92.2 12.9 %copy-start.7 = (s32[128,6]{0,1:T(8,128)S(1)}, s32[128,6]{0,1:T(8,128)}, u32[]{:S(2)}) copy-start(s32[128,6]{0,1:T(8,128)} %param.22) | copy-start | bytes 9220
  93.5 48.0 %all-gather.6.cloned.1.call-start = ((), (), s32[]{:S(2)}) async-start(), calls=%async_computation.5 | async-start | bytes 2359296 | tf_op jit(solution)/shard_map/all_gather | solution.py:103
  101.8 27.0 %copy-start.2 = (bf16[128,1024]{1,0:T(8,128)(2,1)}, bf16[128,1024]{1,0:T(8,128)(2,1)S(1)}, u32[]{:S(2)}) copy-start(bf16[128,1024]{1,0:T(8,128)(2,1)S(1)} %get-tuple-element.3) | copy-start | bytes 786436
  105.1 193.5 %reduce-scatter.5.cloned.1.call-start = ((), (), s32[]{:S(2)}) async-start(), calls=%async_computation.4 | async-start | bytes 2359296 | tf_op jit(solution)/shard_map/reduce_scatter | solution.py:151
  129.2 14.0 %copy-start.5 = (bf16[2048,32]{0,1:T(8,128)(2,1)S(1)}, bf16[2048,32]{0,1:T(8,128)(2,1)}, u32[]{:S(2)}) copy-start(bf16[2048,32]{0,1:T(8,128)(2,1)} %param.26) | copy-start | bytes 393220
  254.6 44.0 %copy-start.1 = (bf16[512,2048]{1,0:T(8,128)(2,1)S(1)}, bf16[512,2048]{1,0:T(8,128)(2,1)}, u32[]{:S(2)}) copy-start(bf16[512,2048]{1,0:T(8,128)(2,1)} %param.24) | copy-start | bytes 6291460
Sparse Core Ops, SparseCore 0:
  9.6 61.2 all-gather.3
  93.6 6.9 reduce-scatter.2
  105.2 31.7 all-gather.5
  261.1 37.4 reduce-scatter.4
where the time goes:
time: 306 us; the launch traced here: 305 us
  local copies, waits for them, and re-layouts  109 us (36%)
  waiting for transfers between devices  66.4 us (22%)
  matrix products  51.3 us (17%)
  blocking collectives  49 us (16%)
  other arithmetic  15.6 us (5%)
  between operations  14.1 us (5%)
    reduce_scatter x1, waiting for transfers between devices, local(): lax.psum_scatter(mixture, ('exp', 'ffn'), scatter_dimension=0, tiled=True)  37.6 us
    all_gather x1, blocking collectives, local(): lax.all_gather(new_latent, 'exp', axis=0, tiled=True)  31.2 us
    gather x3, local copies, waits for them, and re-layouts, local(): chosen = jnp.take_along_axis(logits, routes_all, axis=1)  25.3 us
    all_gather x1, waiting for transfers between devices, local(): lax.all_gather(cache_pool, 'exp', axis=0, tiled=True)  21.1 us
    dot_general x1, matrix products, local(): jnp.einsum('jmf,jfd->jmd', active, down_weight, preferred_element_type=jn...  20.7 us
    gather x1, local copies, waits for them, and re-layouts, local(): normed_grid[slot_token // token_rows, :, slot_token % token_rows, :]  18.4 us
    all_gather x1, blocking collectives, local(): routes_all = lax.all_gather(routes, 'exp', axis=0, tiled=True)  15.2 us
    dot_general x1, matrix products, local(): jnp.einsum('jmd,jdf->jmf', grouped, gate_weight, preferred_element_type=j...  13.1 us
  transfers between devices with their start and end apart: 4, of which 3 were waited for; matrix products, arithmetic and copies ran while one was open for 10% of the time, Pallas kernels for 0%

commit v1 on v0

--- a/solution.py
+++ b/solution.py
@@ -103,7 +103,12 @@
     normed_grid = lax.all_gather(normed_cols, ("exp", "ffn"), axis=0, tiled=False)
     normed_grid = normed_grid.reshape(exp_size, ffn_size, token_rows, column_count)
     group_rows = exp_size * token_rows
-    routes_all = lax.all_gather(routes, "exp", axis=0, tiled=True)
+    ring = [routes]
+    for hop in range(3):
+        ring.append(lax.ppermute(ring[-1], "exp", [(dev, (dev + 1) % 4) for dev in range(4)]))
+    routes_all = jnp.roll(
+        jnp.concatenate(ring[::-1], axis=0), (lax.axis_index("exp") + 1) * ring[0].shape[0], axis=0
+    )
     logits = jnp.einsum(
         "efrc,fck->erk",
         normed_grid,

time: 306 us -> 304 us (level)
  blocking collectives: 49 us -> 33.7 us
  waiting for transfers between devices: 66.4 us -> 77.5 us
    all_gather x1 -> x0, blocking collectives: 15.2 us -> none  [local(): routes_all = lax.all_gather(routes, 'exp', axis=0, tiled=True)]
    ppermute x0 -> x3, waiting for transfers between devices: none -> 14.4 us  [local(): lax.ppermute(ring[-1], 'exp', [(dev, (dev + 1) % 4) for dev in range(4)])]
    reduce_scatter x1, waiting for transfers between devices: 37.6 us -> 34.3 us  [local(): lax.psum_scatter(mixture, ('exp', 'ffn'), scatter_dimension=0, tiled=True)]
  transfers between devices with their start and end apart: 4 -> 7, of which waited for: 3 -> 6; matrix products, arithmetic and copies ran while one was open for 10% -> 10% of each run, Pallas kernels for 0% -> 0%
where the time goes in v1:
time: 304 us; the launch traced here: 303 us
  local copies, waits for them, and re-layouts  109 us (36%)
  waiting for transfers between devices  77.5 us (25%)
  matrix products  51.3 us (17%)
  blocking collectives  33.7 us (11%)
  other arithmetic  15.6 us (5%)
  between operations  14.2 us (5%)
    reduce_scatter x1, waiting for transfers between devices, local(): lax.psum_scatter(mixture, ('exp', 'ffn'), scatter_dimension=0, tiled=True)  34.3 us
    all_gather x1, blocking collectives, local(): lax.all_gather(new_latent, 'exp', axis=0, tiled=True)  31.2 us
    gather x3, local copies, waits for them, and re-layouts, local(): chosen = jnp.take_along_axis(logits, routes_all, axis=1)  25.3 us
    all_gather x1, waiting for transfers between devices, local(): lax.all_gather(cache_pool, 'exp', axis=0, tiled=True)  21.1 us
    dot_general x1, matrix products, local(): jnp.einsum('jmf,jfd->jmd', active, down_weight, preferred_element_type=jn...  20.7 us
    gather x1, local copies, waits for them, and re-layouts, local(): normed_grid[slot_token // token_rows, :, slot_token % token_rows, :]  18.4 us
    ppermute x3, waiting for transfers between devices, local(): lax.ppermute(ring[-1], 'exp', [(dev, (dev + 1) % 4) for dev in range(4)])  14.4 us
    dot_general x1, matrix products, local(): jnp.einsum('jmd,jdf->jmf', grouped, gate_weight, preferred_element_type=j...  13.1 us
  transfers between devices with their start and end apart: 7, of which 6 were waited for; matrix products, arithmetic and copies ran while one was open for 10% of the time, Pallas kernels for 0%

profile of v1, /device:TPU:0, one launch (start us, length us, event | category | flops | bytes accessed | tf_op | source)
XLA Modules:
  0.0 302.8 jit_solution(9561286744292216356)
XLA Ops:
  16.3 31.2 %all_gather.13 = bf16[512,576]{0,1:T(8,128)(2,1)S(1)} all-gather(bf16[128,576]{0,1:T(8,128)(2,1)S(1)} %copy-done.4), channel_id=1, replica_groups=mesh['req'=4,'exp'=4,'ffn'=2] {'exp'}, dimensions={0}, use_global_device_ids=true | all-gather | bytes 737280 | tf_op jit(solution)/shard_map/all_gather | solution.py:57
  49.9 21.1 %all-gather.4.cloned.1.call-done = bf16[128,9216]{1,0:T(8,128)(2,1)} async-done(((bf16[32,9216]{1,0:T(8,128)(2,1)}), bf16[128,9216]{1,0:T(8,128)(2,1)}) %all-gather.4.cloned.1.call-update) | async-done | bytes 2359312 | tf_op jit(solution)/shard_map/all_gather | solution.py:56
  70.9 5.3 %gather_fusion = bf16[64,9216]{1,0:T(8,128)(2,1)} fusion(bf16[128,9216]{1,0:T(8,128)(2,1)} %all-gather.4.cloned.1.call-done, s32[1024]{0:T(1024)S(1)} %pad_clamp_fusion), kind=kCustom, calls=%fused_computation | custom fusion | bytes 2359552 | tf_op jit(solution)/shard_map/jit(_take)/gather | solution.py:61
  76.3 2.2 gather.14
  81.4 3.0 fusion.72
  84.4 3.9 %fusion.5 = f32[128,4,1280]{0,2,1:T(8,128)} fusion(bf16[128,4,576]{0,2,1:T(8,128)(2,1)} %bitcast.110, bf16[256,576]{0,1:T(8,128)(2,1)} %constant_dynamic-slice_fusion.1, bf16[1024,576]{0,1:T(8,128)(2,1)S(1)} %broadcast_select_fusion, pred[128,1280]{0,1:T(8,128)(4,1)S(1)} %copy-done.3), kind=kOutput, calls=%fused_computation.12 | convolution fusion | flops 759234560 | bytes 4849664 | tf_op jit(solution)/shard_map/thd,kd->thk/dot_general | solution.py:69
  88.3 3.9 %fusion.27 = bf16[4,128,128]{1,2,0:T(8,128)(2,1)S(1)} fusion(bf16[512,4,128]{0,2,1:T(8,128)(2,1)} %bitcast.111, bf16[1024,576]{0,1:T(8,128)(2,1)S(1)} %broadcast_select_fusion, bf16[256,576]{0,1:T(8,128)(2,1)} %constant_dynamic-slice_fusion.1, f32[128,4]{0,1:T(4,128)S(1)} %fusion.72, f32[128,4,1280]{0,2,1:T(8,128)} %fusion.5), kind=kOutput, calls=%fused_computation.32 | convolution fusion | flops 743114496 | bytes 7374848 | tf_op jit(solution)/shard_map/thl,lhd->thd/dot_general | solution.py:85
  93.6 7.0 %reduce-scatter.3.cloned.1.call-done = bf16[128,1024]{1,0:T(8,128)(2,1)} async-done(((bf16[128,2048]{1,0:T(8,128)(2,1)}), bf16[128,1024]{1,0:T(8,128)(2,1)}) %reduce-scatter.3.cloned.1.call-update) | async-done | bytes 262160 | tf_op jit(solution)/shard_map/reduce_scatter | solution.py:91
  101.8 2.5 psum.7
  106.9 3.7 %collective-permute-done = s32[128,6]{0,1:T(8,128)S(1)} collective-permute-done((s32[128,6]{0,1:T(8,128)S(1)}, s32[128,6]{0,1:T(8,128)S(1)}, u32[]{:S(2)}, u32[]{:S(2)}) %collective-permute-start) | collective-permute-done | bytes 3104 | tf_op jit(solution)/shard_map/ppermute | solution.py:108
  110.6 5.4 %collective-permute-done.1 = s32[128,6]{0,1:T(8,128)S(1)} collective-permute-done((s32[128,6]{0,1:T(8,128)S(1)}, s32[128,6]{0,1:T(8,128)S(1)}, u32[]{:S(2)}, u32[]{:S(2)}) %collective-permute-start.1) | collective-permute-done | bytes 3104 | tf_op jit(solution)/shard_map/ppermute | solution.py:108
  116.2 5.3 %collective-permute-done.2 = s32[128,6]{0,1:T(8,128)S(1)} collective-permute-done((s32[128,6]{0,1:T(8,128)S(1)}, s32[128,6]{0,1:T(8,128)S(1)}, u32[]{:S(2)}, u32[]{:S(2)}) %collective-permute-start.2) | collective-permute-done | bytes 3104 | tf_op jit(solution)/shard_map/ppermute | solution.py:108
  122.6 6.9 %reduce-window.6 = s32[8,32,3,128]{3,1,2,0:T(8,128)S(1)} reduce-window(s32[8,32,3,128]{3,1,2,0:T(8,128)S(1)} %fusion.38, s32[]{:T(128)} %constant.117.clone.1), window={size=1x1x1x128 pad=0_0x0_0x0_0x127_0}, to_apply=%region_5.6 | reduce-window | flops 12484608 | bytes 786436 | tf_op jit(solution)/shard_map/reduce-window
  130.7 11.8 %scatter_custom_fusion = s32[1024]{0:T(1024)S(1)} fusion(s32[3072]{0:T(1024)S(1)} %bitcast.115, s32[3072]{0:T(1024)S(1)} %reshape.307, s32[]{:T(128)} %constant.117.clone.1), kind=kCustom, calls=%fused_computation.97 | custom fusion | bytes 4100 | tf_op jit(solution)/shard_map/scatter | solution.py:132
  145.0 24.9 %gather_fusion.2 = f32[3072]{0:T(1024)S(1)} fusion(f32[512,32]{0,1:T(8,128)S(1)} %convolution_bitcast_fusion, s32[3072]{0:T(1024)S(1)} %reshape.297), kind=kCustom, calls=%fused_computation.2 | custom fusion | bytes 49152 | tf_op jit(solution)/shard_map/jit(take_along_axis)/gather | solution.py:118
  170.6 5.1 %copy.46 = bf16[4,2,128,1024]{3,1,2,0:T(2,128)(2,1)} copy(bf16[4,2,128,1024]{3,2,1,0:T(8,128)(2,1)} %bitcast.105) | data formatting | bytes 4194304 | tf_op jit(solution)/shard_map/reshape | solution.py:104
  175.7 18.4 %gather_fusion.1 = bf16[1024,2,1024]{2,1,0:T(2,128)(2,1)} fusion(bf16[4,2,128,1024]{3,1,2,0:T(2,128)(2,1)} %copy.46, s32[1024]{0:T(1024)S(1)} %fusion.49), kind=kCustom, calls=%fused_computation.1 | custom fusion | bytes 8396800 | tf_op jit(solution)/shard_map/gather | solution.py:138
  194.2 7.8 %reshape.279 = bf16[8,128,2048]{2,1,0:T(8,128)(2,1)} reshape(bf16[1024,2,1024]{2,1,0:T(2,128)(2,1)} %gather_fusion.1) | data formatting | bytes 8388608 | tf_op jit(solution)/shard_map/reshape | solution.py:139
  202.0 12.0 %scatter_custom_fusion.1 = f32[1024]{0:T(1024)S(1)} fusion(s32[3072]{0:T(1024)S(1)} %bitcast.116, f32[3072]{0:T(1024)S(1)} %reshape.315, f32[]{:T(128)} %constant.137.clone.1), kind=kCustom, calls=%fused_computation.100 | custom fusion | bytes 4100 | tf_op jit(solution)/shard_map/scatter | solution.py:136
  214.0 13.1 %fusion.75 = f32[8,128,704]{1,2,0:T(8,128)} fusion(bf16[8,128,2048]{2,1,0:T(8,128)(2,1)} %reshape.279, bf16[8,2048,704]{1,2,0:T(8,128)(2,1)} %param.27), kind=kOutput, calls=%fused_computation.120 | convolution fusion | flops 2952790016 | bytes 30146560 | tf_op jit(solution)/shard_map/jmd,jdf->jmf/dot_general | solution.py:140
  227.1 20.7 %multiply_convert_fusion = bf16[8,128,2048]{2,1,0:T(8,128)(2,1)} fusion(f32[8,128]{1,0:T(8,128)S(1)} %bitcast.117, bf16[8,704,2048]{2,1,0:T(8,128)(2,1)} %param.29, f32[8,128,704]{1,2,0:T(8,128)} %fusion.75, bf16[8,128,2048]{2,1,0:T(8,128)(2,1)} %reshape.279, bf16[8,2048,704]{1,2,0:T(8,128)(2,1)} %param.28), kind=kOutput, calls=%fused_computation.6 | convolution fusion | flops 5914099712 | bytes 57413632 | tf_op jit(solution)/shard_map/jmf,jfd->jmd/dot_general | solution.py:143
  247.8 7.8 %convert_element_type.72 = bf16[1024,2,1024]{2,1,0:T(2,128)(2,1)} reshape(bf16[8,128,2048]{2,1,0:T(8,128)(2,1)} %multiply_convert_fusion) | data formatting | bytes 8388608 | tf_op jit(solution)/shard_map/convert_element_type | solution.py:144
  255.5 4.8 %convert_bitcast_fusion = bf16[4,2,128,1024]{3,2,0,1:T(8,128)(2,1)S(1)} fusion(bf16[1024,2,1024,1]{2,1,0,3:T(2,128)(2,1)} %bitcast.108, s32[4,128]{1,0:T(4,128)S(1)} %multiply_add_fusion, s32[1024]{0:T(1024)S(1)} %scatter_custom_fusion), kind=kOutput, calls=%fused_computation.17 | convolution fusion | flops 2149056512 | bytes 6297600 | tf_op jit(solution)/shard_map/ers,sfc->efrc/dot_general | solution.py:149
  262.0 34.3 %reduce-scatter.5.cloned.1.call-done = bf16[128,1024]{1,0:T(8,128)(2,1)} async-done(((bf16[1024,1024]{1,0:T(8,128)(2,1)}), bf16[128,1024]{1,0:T(8,128)(2,1)}) %reduce-scatter.5.cloned.1.call-update) | async-done | bytes 262160 | tf_op jit(solution)/shard_map/reduce_scatter | solution.py:156
  (95 shorter events, 26.5 us)
Async XLA Ops:
  7.2 85.1 %copy-start = (bf16[512,2048]{1,0:T(8,128)(2,1)S(1)}, bf16[512,2048]{1,0:T(8,128)(2,1)}, u32[]{:S(2)}) copy-start(bf16[512,2048]{1,0:T(8,128)(2,1)} %param.24) | copy-start | bytes 6291460
  7.2 5.9 %copy-start.9 = (s32[8]{0:T(128)S(1)}, s32[8]{0:T(128)}, u32[]{:S(2)}) copy-start(s32[8]{0:T(128)} %param.20) | copy-start | bytes 100
  7.2 6.5 %copy-start.10 = (s32[8]{0:T(128)S(1)}, s32[8]{0:T(128)}, u32[]{:S(2)}) copy-start(s32[8]{0:T(128)} %param.21) | copy-start | bytes 100
  7.2 9.1 %copy-start.4 = (bf16[128,576]{0,1:T(8,128)(2,1)S(1)}, bf16[128,576]{0,1:T(8,128)(2,1)}, u32[]{:S(2)}) copy-start(bf16[128,576]{0,1:T(8,128)(2,1)} %param.17) | copy-start | bytes 442372
  7.2 63.7 %all-gather.4.cloned.1.call-start = ((), (), s32[]{:S(2)}) async-start(), calls=%async_computation.2 | async-start | bytes 2949120 | tf_op jit(solution)/shard_map/all_gather | solution.py:56
  7.9 92.7 %reduce-scatter.3.cloned.1.call-start = ((), (), s32[]{:S(2)}) async-start(), calls=%async_computation.3 | async-start | bytes 786432 | tf_op jit(solution)/shard_map/reduce_scatter | solution.py:91
  81.4 3.0 copy-start.3
  92.2 1.4 copy-start.8
  92.2 8.4 %copy-start.6 = (bf16[128,2048]{1,0:T(8,128)(2,1)S(1)}, bf16[128,2048]{1,0:T(8,128)(2,1)}, u32[]{:S(2)}) copy-start(bf16[128,2048]{1,0:T(8,128)(2,1)} %param.15) | copy-start | bytes 1572868
  92.2 12.9 %copy-start.7 = (s32[128,6]{0,1:T(8,128)S(1)}, s32[128,6]{0,1:T(8,128)}, u32[]{:S(2)}) copy-start(s32[128,6]{0,1:T(8,128)} %param.22) | copy-start | bytes 9220
  93.5 49.0 %all-gather.6.cloned.1.call-start = ((), (), s32[]{:S(2)}) async-start(), calls=%async_computation.5 | async-start | bytes 2359296 | tf_op jit(solution)/shard_map/all_gather | solution.py:103
  101.8 28.0 %copy-start.2 = (bf16[128,1024]{1,0:T(8,128)(2,1)}, bf16[128,1024]{1,0:T(8,128)(2,1)S(1)}, u32[]{:S(2)}) copy-start(bf16[128,1024]{1,0:T(8,128)(2,1)S(1)} %get-tuple-element.3) | copy-start | bytes 786436
  105.1 191.2 %reduce-scatter.5.cloned.1.call-start = ((), (), s32[]{:S(2)}) async-start(), calls=%async_computation.4 | async-start | bytes 2359296 | tf_op jit(solution)/shard_map/reduce_scatter | solution.py:156
  105.2 5.5 %collective-permute-start = (s32[128,6]{0,1:T(8,128)S(1)}, s32[128,6]{0,1:T(8,128)S(1)}, u32[]{:S(2)}, u32[]{:S(2)}) collective-permute-start(s32[128,6]{0,1:T(8,128)S(1)} %copy-done.7), channel_id=1, source_target_pairs={{0,2},{2,4},{4,6},{6,0},{1,3},{3,5},{5,7},{7,1},{8,10},{10,12},{12... | collective-permute-start | bytes 9224 | tf_op jit(solution)/shard_map/ppermute | solution.py:108
  110.6 5.4 %collective-permute-start.1 = (s32[128,6]{0,1:T(8,128)S(1)}, s32[128,6]{0,1:T(8,128)S(1)}, u32[]{:S(2)}, u32[]{:S(2)}) collective-permute-start(s32[128,6]{0,1:T(8,128)S(1)} %collective-permute-done), channel_id=1, source_target_pairs={{0,2},{2,4},{4,6},{6,0},{1,3},{3,5},{5,7},{7,1},{8,10},{10,12},{12... | collective-permute-start | bytes 9224 | tf_op jit(solution)/shard_map/ppermute | solution.py:108
  116.0 5.5 %collective-permute-start.2 = (s32[128,6]{0,1:T(8,128)S(1)}, s32[128,6]{0,1:T(8,128)S(1)}, u32[]{:S(2)}, u32[]{:S(2)}) collective-permute-start(s32[128,6]{0,1:T(8,128)S(1)} %collective-permute-done.1), channel_id=1, source_target_pairs={{0,2},{2,4},{4,6},{6,0},{1,3},{3,5},{5,7},{7,1},{8,10},{10,12},{12... | collective-permute-start | bytes 9224 | tf_op jit(solution)/shard_map/ppermute | solution.py:108
  130.2 14.0 %copy-start.5 = (bf16[2048,32]{0,1:T(8,128)(2,1)S(1)}, bf16[2048,32]{0,1:T(8,128)(2,1)}, u32[]{:S(2)}) copy-start(bf16[2048,32]{0,1:T(8,128)(2,1)} %param.26) | copy-start | bytes 393220
  255.5 40.7 %copy-start.1 = (bf16[512,2048]{1,0:T(8,128)(2,1)S(1)}, bf16[512,2048]{1,0:T(8,128)(2,1)}, u32[]{:S(2)}) copy-start(bf16[512,2048]{1,0:T(8,128)(2,1)} %param.24) | copy-start | bytes 6291460
Sparse Core Ops, SparseCore 0:
  9.6 61.2 all-gather.3
  93.6 6.9 reduce-scatter.2
  105.2 30.2 all-gather.5
  262.1 34.1 reduce-scatter.4
